TPU v7x, 256 devices: a whole 4x4x8 slice. The times are simulated.
256 devices in a mesh: layer: 64 (over y, z, core), blk: 4 (over x).
Axes of the slice: x: 4, y: 4, z: 8, core: 2. Of those that a mesh axis runs over, the one named last changes fastest.
Arguments:
- mode_matrix: bfloat16 [128, 512, 512], P(None, 'layer', 'blk'), may hold values from -1 to 1, as said below
- decay_rate: bfloat16 [128, 512], P(None, 'layer'), may hold values from 0.0009994507 to 0.29882812
- facet_refl: bfloat16 [128, 512], P(None, 'layer'), may hold values from -0.796875 to 0.796875
Outputs:
- prefix: bfloat16 [64, 4, 512, 512], P('layer', None, 'blk')
Inputs may be any that keep to these rules, and one draw needn't show every extreme that they name: `mode_matrix`: each layer's matrix has orthonormal columns up to the rounding to bfloat16.
All inputs are finite; a program needn't handle non-finite values.
Results may differ from a plain program's by a relative error of at most 0.0045.
The roundings to bfloat16 on the way count: a program that leaves them out, or rounds other values in their place, can miss the bound.
Values may be sent and summed in bfloat16 or wider, within the bound.
No kernel may reach another device: no remote copies, remote signals or barrier semaphores. Data moves between devices by JAX's collectives and lax.ppermute only.
A program may use at most 64 MiB of HBM per device.

v0:
```python
import jax
import jax.numpy as jnp
from jax import lax
from jax.sharding import PartitionSpec as P

HARM = 512
REFL = 4


def passed_along(value, axis, steps):
    count = lax.axis_size(axis)
    first, last = (max(0, -steps), min(count, count - steps))
    return lax.ppermute(value, axis, [(source, source + steps) for source in range(first, last)])


def times_f32(left_op, right_op):
    return jnp.dot(left_op, right_op, preferred_element_type=jnp.float32)


def star_rows(upper_near, upper_far, lower_near, lower_rows):
    coupling_down = times_f32(lower_near[0], upper_far[1]).astype(jnp.bfloat16)
    coupling_up = times_f32(upper_far[1], lower_near[0]).astype(jnp.bfloat16)
    left_sum = upper_near[1]
    for repeat in range(REFL):
        left_sum = (upper_near[1] + times_f32(left_sum, coupling_down)).astype(jnp.bfloat16)
    right_sum = lower_rows[0]
    for repeat in range(REFL):
        right_sum = (lower_rows[0] + times_f32(right_sum, coupling_up)).astype(jnp.bfloat16)
    left_mid = times_f32(left_sum, lower_near[0]).astype(jnp.bfloat16)
    right_mid = times_f32(right_sum, upper_far[1]).astype(jnp.bfloat16)
    new_refl = (upper_near[0] + times_f32(left_mid, upper_far[0])).astype(jnp.bfloat16)
    new_back = times_f32(left_sum, lower_near[1]).astype(jnp.bfloat16)
    new_fore = times_f32(right_sum, upper_far[0]).astype(jnp.bfloat16)
    new_under = (lower_rows[1] + times_f32(right_mid, lower_near[1])).astype(jnp.bfloat16)
    return jnp.stack([new_refl, new_back, new_fore, new_under])


def on_device(mode_matrix, decay_rate, facet_refl):
    relayed_modes, relayed_decay, relayed_refl = (
        lax.all_to_all(mode_matrix, "layer", split_axis=0, concat_axis=1, tiled=True),
        lax.all_to_all(decay_rate, "layer", split_axis=0, concat_axis=1, tiled=True),
        lax.all_to_all(facet_refl, "layer", split_axis=0, concat_axis=1, tiled=True),
    )
    block_index = lax.axis_index("blk")
    row_count = HARM // lax.axis_size("blk")
    row_start = block_index * row_count
    refl_full = relayed_refl.astype(jnp.float32)
    transmit = jnp.sqrt(1.0 - refl_full * refl_full) * jnp.exp(-relayed_decay.astype(jnp.float32))
    mode_piece = lax.all_gather(relayed_modes, "blk", axis=2, tiled=True)
    piece_wide = mode_piece.astype(jnp.float32)
    scaled_refl = (piece_wide * refl_full[:, None, :]).astype(jnp.bfloat16)
    scaled_tran = (piece_wide * transmit[:, None, :]).astype(jnp.bfloat16)
    own_rows = lax.dynamic_slice_in_dim(mode_piece, row_start, row_count, 1)
    refl_part = jnp.einsum(
        "lhm,lkm->lhk", own_rows, scaled_refl, preferred_element_type=jnp.float32
    )
    tran_part = jnp.einsum(
        "lhm,lkm->lhk", own_rows, scaled_tran, preferred_element_type=jnp.float32
    )
    refl_rows = refl_part.astype(jnp.bfloat16)
    tran_rows = tran_part.astype(jnp.bfloat16)
    layer_rows = jnp.stack([refl_rows, tran_rows, tran_rows, -refl_rows], axis=1)
    layer_pair = lax.all_gather(
        jnp.stack([refl_rows, tran_rows], axis=1), "blk", axis=2, tiled=True
    )
    rows_now = layer_rows[0]
    full_now = jnp.stack([layer_pair[0, 0], layer_pair[0, 1], layer_pair[0, 1], -layer_pair[0, 0]])
    rows_now = star_rows(rows_now[0:2], full_now[2:4], layer_pair[1], layer_rows[1, 2:4])
    full_now = lax.all_gather(rows_now, "blk", axis=1, tiled=True)
    group_index = lax.axis_index("layer")
    level_count = lax.axis_size("layer").bit_length() - 1
    for section_level in range(level_count):
        distance = 1 << section_level
        upper_whole = passed_along(full_now, "layer", distance)
        upper_near = lax.dynamic_slice_in_dim(upper_whole[0:2], row_start, row_count, 1)
        upper_far = upper_whole[2:4]
        combined = star_rows(upper_near, upper_far, full_now[0:2], rows_now[2:4])
        rows_now = jnp.where(group_index >= distance, combined, rows_now)
        if section_level + 1 < level_count:
            full_now = lax.all_gather(rows_now, "blk", axis=1, tiled=True)
    return rows_now[None]


def solution(mesh):
    placed = (P(None, "layer", "blk"), P(None, "layer"), P(None, "layer"))
    return jax.shard_map(
        on_device,
        mesh=mesh,
        in_specs=placed,
        out_specs=P("layer", None, "blk", None),
        check_vma=False,
    )
```

profile of v0, /device:TPU:16, one launch (start us, length us, event | category | flops | bytes accessed | tf_op | source)
XLA Modules:
  0.0 783.8 jit_solution(11975169473791905162)
XLA Ops:
  6.5 23.6 %all_to_all.44 = bf16[128,8,128]{2,1,0:T(8,128)(2,1)S(1)} all-to-all(bf16[128,8,128]{2,1,0:T(8,128)(2,1)} %param.3), channel_id=1, replica_groups=mesh['layer'=64,'blk'=4] {'layer'}, dimensions={0} | all-to-all | bytes 524288 | tf_op jit(solution)/shard_map/all_to_all | solution.py:40
  32.3 6.5 all-to-all-start.1
  40.2 6.3 all-to-all-done.1
  46.5 6.4 all-to-all-start.2
  53.1 7.5 all-to-all-done.2
  65.5 30.2 %all-gather.11.cloned.1.call-done = bf16[2,2,512,512]{3,2,0,1:T(8,128)(2,1)} async-done(((bf16[2,2,128,512]{3,2,0,1:T(8,128)(2,1)}), bf16[2,2,512,512]{3,2,0,1:T(8,128)(2,1)}) %all-gather.11.cloned.1.call-update) | async-done | bytes 2097168 | tf_op jit(solution)/shard_map/all_gather | solution.py:63
  101.8 33.5 %all-gather.13.cloned.1.call-done = bf16[4,512,512]{2,1,0:T(8,128)(2,1)} async-done(((bf16[4,128,512]{2,1,0:T(8,128)(2,1)}), bf16[4,512,512]{2,1,0:T(8,128)(2,1)}) %all-gather.13.cloned.1.call-update) | async-done | bytes 2097168 | tf_op jit(solution)/shard_map/all_gather | solution.py:69
  137.3 27.7 %collective-permute-done = bf16[4,512,512]{2,1,0:T(8,128)(2,1)S(1)} collective-permute-done((bf16[4,512,512]{2,1,0:T(8,128)(2,1)}, bf16[4,512,512]{2,1,0:T(8,128)(2,1)S(1)}, u32[]{:S(2)}, u32[]{:S(2)}) %collective-permute-start) | collective-permute-done | bytes 2097184 | tf_op jit(solution)/shard_map/ppermute | solution.py:13
  178.0 32.6 %all-gather.15.cloned.1.call-done = bf16[4,512,512]{2,1,0:T(8,128)(2,1)} async-done(((bf16[4,128,512]{2,1,0:T(8,128)(2,1)}), bf16[4,512,512]{2,1,0:T(8,128)(2,1)}) %all-gather.15.cloned.1.call-update) | async-done | bytes 2097168 | tf_op jit(solution)/shard_map/all_gather | solution.py:80
  210.7 3.5 collective-permute-start.1
  214.1 48.2 %collective-permute-done.1 = bf16[4,512,512]{2,1,0:T(8,128)(2,1)} collective-permute-done((bf16[4,512,512]{2,1,0:T(8,128)(2,1)}, bf16[4,512,512]{2,1,0:T(8,128)(2,1)}, u32[]{:S(2)}, u32[]{:S(2)}) %collective-permute-start.1) | collective-permute-done | bytes 2097184 | tf_op jit(solution)/shard_map/ppermute | solution.py:13
  275.4 32.6 %all-gather.17.cloned.1.call-done = bf16[4,512,512]{2,1,0:T(8,128)(2,1)} async-done(((bf16[4,128,512]{2,1,0:T(8,128)(2,1)}), bf16[4,512,512]{2,1,0:T(8,128)(2,1)}) %all-gather.17.cloned.1.call-update) | async-done | bytes 2097168 | tf_op jit(solution)/shard_map/all_gather | solution.py:80
  308.1 4.6 collective-permute-start.2
  312.7 93.8 %collective-permute-done.2 = bf16[4,512,512]{2,1,0:T(8,128)(2,1)} collective-permute-done((bf16[4,512,512]{2,1,0:T(8,128)(2,1)}, bf16[4,512,512]{2,1,0:T(8,128)(2,1)}, u32[]{:S(2)}, u32[]{:S(2)}) %collective-permute-start.2) | collective-permute-done | bytes 2097184 | tf_op jit(solution)/shard_map/ppermute | solution.py:13
  421.0 32.6 %all-gather.19.cloned.1.call-done = bf16[4,512,512]{2,1,0:T(8,128)(2,1)} async-done(((bf16[4,128,512]{2,1,0:T(8,128)(2,1)}), bf16[4,512,512]{2,1,0:T(8,128)(2,1)}) %all-gather.19.cloned.1.call-update) | async-done | bytes 2097168 | tf_op jit(solution)/shard_map/all_gather | solution.py:80
  453.6 7.6 collective-permute-start.3
  461.3 80.8 %collective-permute-done.3 = bf16[4,512,512]{2,1,0:T(8,128)(2,1)} collective-permute-done((bf16[4,512,512]{2,1,0:T(8,128)(2,1)}, bf16[4,512,512]{2,1,0:T(8,128)(2,1)}, u32[]{:S(2)}, u32[]{:S(2)}) %collective-permute-start.3) | collective-permute-done | bytes 2097184 | tf_op jit(solution)/shard_map/ppermute | solution.py:13
  559.2 44.1 %all-gather.21.cloned.1.call-done = bf16[4,512,512]{2,1,0:T(8,128)(2,1)} async-done(((bf16[4,128,512]{2,1,0:T(8,128)(2,1)}), bf16[4,512,512]{2,1,0:T(8,128)(2,1)}) %all-gather.21.cloned.1.call-update) | async-done | bytes 2097168 | tf_op jit(solution)/shard_map/all_gather | solution.py:80
  603.4 3.1 collective-permute-start.4
  606.5 46.5 %collective-permute-done.4 = bf16[4,512,512]{2,1,0:T(8,128)(2,1)} collective-permute-done((bf16[4,512,512]{2,1,0:T(8,128)(2,1)}, bf16[4,512,512]{2,1,0:T(8,128)(2,1)}, u32[]{:S(2)}, u32[]{:S(2)}) %collective-permute-start.4) | collective-permute-done | bytes 2097184 | tf_op jit(solution)/shard_map/ppermute | solution.py:13
  662.0 2.4 fusion.32
  672.9 33.6 %all-gather.23.cloned.1.call-done = bf16[4,512,512]{2,1,0:T(8,128)(2,1)} async-done(((bf16[4,128,512]{2,1,0:T(8,128)(2,1)}), bf16[4,512,512]{2,1,0:T(8,128)(2,1)}) %all-gather.23.cloned.1.call-update) | async-done | bytes 2097168 | tf_op jit(solution)/shard_map/all_gather | solution.py:80
  707.7 49.8 %collective-permute-done.5 = bf16[4,512,512]{2,1,0:T(8,128)(2,1)} collective-permute-done((bf16[4,512,512]{2,1,0:T(8,128)(2,1)}, bf16[4,512,512]{2,1,0:T(8,128)(2,1)}, u32[]{:S(2)}, u32[]{:S(2)}) %collective-permute-start.5) | collective-permute-done | bytes 2097184 | tf_op jit(solution)/shard_map/ppermute | solution.py:13
  766.6 2.4 fusion.68
  (160 shorter events, 109.6 us)
Async XLA Ops:
  6.5 54.4 %all-gather.9.cloned.1.call-start = ((), (), s32[]{:S(2)}) async-start(), calls=%async_computation.3 | async-start | bytes 1310720 | tf_op jit(solution)/shard_map/all_gather | solution.py:49
  32.3 14.2 %all-to-all-start.1 = ((bf16[64,2,8]{2,1,0:T(2,128)(2,1)}), bf16[64,2,8]{2,1,0:T(2,128)(2,1)S(1)}, u32[]{:S(2)}, u32[]{:S(2)}) async-start(bf16[64,2,8]{2,1,0:T(2,128)(2,1)} %bitcast.3), calls=%async_computation.1 | async-start | bytes 65536 | tf_op jit(solution)/shard_map/all_to_all | solution.py:42
  46.5 14.1 %all-to-all-start.2 = ((bf16[64,2,8]{2,1,0:T(2,128)(2,1)}), bf16[64,2,8]{2,1,0:T(2,128)(2,1)S(1)}, u32[]{:S(2)}, u32[]{:S(2)}) async-start(bf16[64,2,8]{2,1,0:T(2,128)(2,1)} %bitcast.6), calls=%async_computation.2 | async-start | bytes 65536 | tf_op jit(solution)/shard_map/all_to_all | solution.py:41
  52.9 42.8 %all-gather.11.cloned.1.call-start = ((), (), s32[]{:S(2)}) async-start(), calls=%async_computation.4 | async-start | bytes 2621440 | tf_op jit(solution)/shard_map/all_gather | solution.py:63
  65.4 69.9 %all-gather.13.cloned.1.call-start = ((), (), s32[]{:S(2)}) async-start(), calls=%async_computation.5 | async-start | bytes 2621440 | tf_op jit(solution)/shard_map/all_gather | solution.py:69
  101.7 108.9 %all-gather.15.cloned.1.call-start = ((), (), s32[]{:S(2)}) async-start(), calls=%async_computation.6 | async-start | bytes 2621440 | tf_op jit(solution)/shard_map/all_gather | solution.py:80
  135.3 29.7 %collective-permute-start = (bf16[4,512,512]{2,1,0:T(8,128)(2,1)}, bf16[4,512,512]{2,1,0:T(8,128)(2,1)S(1)}, u32[]{:S(2)}, u32[]{:S(2)}) collective-permute-start(bf16[4,512,512]{2,1,0:T(8,128)(2,1)} %all-gather.13.cloned.1.call-done), channel_id=1, source_target_pairs={{0,4},{4,8},{8,12},{12,16},{16,20},{20,24},{24,28},{28,32},{32,36}... | collective-permute-start | bytes 6291464 | tf_op jit(solution)/shard_map/ppermute | solution.py:13
  178.0 86.0 %copy-start.1 = (bf16[4,128,512]{2,1,0:T(8,128)(2,1)S(1)}, bf16[4,128,512]{2,1,0:T(8,128)(2,1)}, u32[]{:S(2)}) copy-start(bf16[4,128,512]{2,1,0:T(8,128)(2,1)} %maximum_select_fusion) | copy-start | bytes 1572868
  178.0 130.1 %all-gather.17.cloned.1.call-start = ((), (), s32[]{:S(2)}) async-start(), calls=%async_computation.7 | async-start | bytes 2621440 | tf_op jit(solution)/shard_map/all_gather | solution.py:80
  210.7 51.7 %collective-permute-start.1 = (bf16[4,512,512]{2,1,0:T(8,128)(2,1)}, bf16[4,512,512]{2,1,0:T(8,128)(2,1)}, u32[]{:S(2)}, u32[]{:S(2)}) collective-permute-start(bf16[4,512,512]{2,1,0:T(8,128)(2,1)} %all-gather.15.cloned.1.call-done), channel_id=1, source_target_pairs={{0,8},{4,12},{8,16},{12,20},{16,24},{20,28},{24,32},{28,36},{32,40... | collective-permute-start | bytes 6291464 | tf_op jit(solution)/shard_map/ppermute | solution.py:13
  275.4 132.7 %copy-start.2 = (bf16[4,128,512]{2,1,0:T(8,128)(2,1)S(1)}, bf16[4,128,512]{2,1,0:T(8,128)(2,1)}, u32[]{:S(2)}) copy-start(bf16[4,128,512]{2,1,0:T(8,128)(2,1)} %maximum_select_fusion.1) | copy-start | bytes 1572868
  275.4 178.2 %all-gather.19.cloned.1.call-start = ((), (), s32[]{:S(2)}) async-start(), calls=%async_computation.8 | async-start | bytes 2621440 | tf_op jit(solution)/shard_map/all_gather | solution.py:80
  308.1 98.4 %collective-permute-start.2 = (bf16[4,512,512]{2,1,0:T(8,128)(2,1)}, bf16[4,512,512]{2,1,0:T(8,128)(2,1)}, u32[]{:S(2)}, u32[]{:S(2)}) collective-permute-start(bf16[4,512,512]{2,1,0:T(8,128)(2,1)} %all-gather.17.cloned.1.call-done), channel_id=1, source_target_pairs={{0,16},{4,20},{8,24},{12,28},{16,32},{20,36},{24,40},{28,44},{32,4... | collective-permute-start | bytes 6291464 | tf_op jit(solution)/shard_map/ppermute | solution.py:13
  420.9 122.8 %copy-start.3 = (bf16[4,128,512]{2,1,0:T(8,128)(2,1)S(1)}, bf16[4,128,512]{2,1,0:T(8,128)(2,1)}, u32[]{:S(2)}) copy-start(bf16[4,128,512]{2,1,0:T(8,128)(2,1)} %maximum_select_fusion.2) | copy-start | bytes 1572868
  420.9 182.4 %all-gather.21.cloned.1.call-start = ((), (), s32[]{:S(2)}) async-start(), calls=%async_computation.9 | async-start | bytes 2621440 | tf_op jit(solution)/shard_map/all_gather | solution.py:80
  453.6 88.5 %collective-permute-start.3 = (bf16[4,512,512]{2,1,0:T(8,128)(2,1)}, bf16[4,512,512]{2,1,0:T(8,128)(2,1)}, u32[]{:S(2)}, u32[]{:S(2)}) collective-permute-start(bf16[4,512,512]{2,1,0:T(8,128)(2,1)} %all-gather.19.cloned.1.call-done), channel_id=1, source_target_pairs={{0,32},{4,36},{8,40},{12,44},{16,48},{20,52},{24,56},{28,60},{32,6... | collective-permute-start | bytes 6291464 | tf_op jit(solution)/shard_map/ppermute | solution.py:13
  559.1 95.4 %copy-start.4 = (bf16[4,128,512]{2,1,0:T(8,128)(2,1)S(1)}, bf16[4,128,512]{2,1,0:T(8,128)(2,1)}, u32[]{:S(2)}) copy-start(bf16[4,128,512]{2,1,0:T(8,128)(2,1)} %maximum_select_fusion.3) | copy-start | bytes 1572868
  559.2 147.3 %all-gather.23.cloned.1.call-start = ((), (), s32[]{:S(2)}) async-start(), calls=%async_computation.10 | async-start | bytes 2621440 | tf_op jit(solution)/shard_map/all_gather | solution.py:80
  603.4 49.6 %collective-permute-start.4 = (bf16[4,512,512]{2,1,0:T(8,128)(2,1)}, bf16[4,512,512]{2,1,0:T(8,128)(2,1)}, u32[]{:S(2)}, u32[]{:S(2)}) collective-permute-start(bf16[4,512,512]{2,1,0:T(8,128)(2,1)} %all-gather.21.cloned.1.call-done), channel_id=1, source_target_pairs={{0,64},{4,68},{8,72},{12,76},{16,80},{20,84},{24,88},{28,92},{32,9... | collective-permute-start | bytes 6291464 | tf_op jit(solution)/shard_map/ppermute | solution.py:13
  662.0 8.7 %copy-start.10 = (bf16[128,512]{1,0:T(8,128)(2,1)S(1)}, bf16[128,512]{1,0:T(8,128)(2,1)}, u32[]{:S(2)}) copy-start(bf16[128,512]{1,0:T(8,128)(2,1)} %copy-done.9) | copy-start | bytes 393220
  662.0 8.7 %copy-start.13 = (bf16[128,512]{1,0:T(8,128)(2,1)S(1)}, bf16[128,512]{1,0:T(8,128)(2,1)}, u32[]{:S(2)}) copy-start(bf16[128,512]{1,0:T(8,128)(2,1)} %copy-done.12) | copy-start | bytes 393220
  662.0 8.7 %copy-start.16 = (bf16[128,512]{1,0:T(8,128)(2,1)S(1)}, bf16[128,512]{1,0:T(8,128)(2,1)}, u32[]{:S(2)}) copy-start(bf16[128,512]{1,0:T(8,128)(2,1)} %copy-done.15) | copy-start | bytes 393220
  672.8 86.3 %copy-start = (bf16[4,128,512]{2,1,0:T(8,128)(2,1)S(1)}, bf16[4,128,512]{2,1,0:T(8,128)(2,1)}, u32[]{:S(2)}) copy-start(bf16[4,128,512]{2,1,0:T(8,128)(2,1)} %maximum_select_fusion.4) | copy-start | bytes 1572868
  706.4 51.1 %collective-permute-start.5 = (bf16[4,512,512]{2,1,0:T(8,128)(2,1)}, bf16[4,512,512]{2,1,0:T(8,128)(2,1)}, u32[]{:S(2)}, u32[]{:S(2)}) collective-permute-start(bf16[4,512,512]{2,1,0:T(8,128)(2,1)} %all-gather.23.cloned.1.call-done), channel_id=1, source_target_pairs={{0,128},{4,132},{8,136},{12,140},{16,144},{20,148},{24,152},{28,15... | collective-permute-start | bytes 6291464 | tf_op jit(solution)/shard_map/ppermute | solution.py:13
  (15 other events, 72.3 us)
Sparse Core Ops, SparseCore 0:
  31.0 25.5 all-gather.8
  65.5 30.0 all-gather.10
  101.9 33.4 all-gather.12
  178.1 32.5 all-gather.14
  275.5 32.5 all-gather.16
  421.0 32.5 all-gather.18
  559.3 44.0 all-gather.20
  673.0 33.4 all-gather.22
where the time goes:
time: 786 us; the launch traced here: 784 us
  waiting for transfers between devices  600 us (76%)
  matrix products  86.9 us (11%)
  starting transfers between devices  35.1 us (4%)
  blocking collectives  23.6 us (3%)
  between operations  14.3 us (2%)
  local copies, waits for them, and re-layouts  13.7 us (2%)
  other arithmetic  10.2 us (1%)
    ppermute x6, waiting for transfers between devices, passed_along(): lax.ppermute(value, axis, [(source, source + steps) for source in range(f...  347 us
    all_gather x6, waiting for transfers between devices, on_device(): full_now = lax.all_gather(rows_now, 'blk', axis=1, tiled=True)  209 us
    dot_general x70, matrix products, times_f32(): return jnp.dot(left_op, right_op, preferred_element_type=jnp.float32)  83.3 us
    all_gather x1, waiting for transfers between devices, on_device(): lax.all_gather(jnp.stack([refl_rows, tran_rows], axis=1), 'blk', axis=2,...  30.2 us
    all_to_all x1, blocking collectives, on_device(): lax.all_to_all(mode_matrix, 'layer', split_axis=0, concat_axis=1, tiled=T...  23.6 us
    ppermute x6, starting transfers between devices, passed_along(): lax.ppermute(value, axis, [(source, source + steps) for source in range(f...  22 us
  transfers between devices with their start and end apart: 16, of which 15 were waited for; matrix products, arithmetic and copies ran while one was open for 0% of the time, Pallas kernels for 0%

commit v1 on v0

--- a/solution.py
+++ b/solution.py
@@ -1,3 +1,4 @@
+import functools
 import jax
 import jax.numpy as jnp
 from jax import lax
@@ -5,6 +6,36 @@
 
 HARM = 512
 REFL = 4
+
+
+def wrap_series_all(buf, link_axis, pos_dim):
+    out_arr = jax.lax.axis_size(link_axis)
+    y1 = jax.lax.axis_index(link_axis)
+    d_next, long_array, newest = (out_arr, y1, buf.shape[pos_dim])
+    z2 = range(d_next)
+    formed = map(lambda at: (at, (at + 1) % d_next), z2)
+    so_far_all = list(formed)
+    even = range(d_next)
+    b_now = map(lambda at: (at, (at - 1) % d_next), even)
+    pool = list(b_now)
+    z1 = jnp.zeros((*buf.shape[:pos_dim], d_next * newest, *buf.shape[pos_dim + 1 :]), buf.dtype)
+    z1 = lax.dynamic_update_slice_in_dim(z1, buf, long_array * newest, axis=pos_dim)
+    f_next = frame_out = buf
+    raw_out = d_next // 2
+    for c in range(1, raw_out + 1):
+        f_next = jax.lax.ppermute(f_next, link_axis, so_far_all)
+        z1 = lax.dynamic_update_slice_in_dim(
+            z1, f_next, (long_array - c) % d_next * newest, axis=pos_dim
+        )
+        if c < d_next - raw_out:
+            frame_out = jax.lax.ppermute(frame_out, link_axis, pool)
+            z1 = lax.dynamic_update_slice_in_dim(
+                z1, frame_out, (long_array + c) % d_next * newest, axis=pos_dim
+            )
+    return z1
+
+
+assign_files = functools.partial(wrap_series_all, link_axis="blk", pos_dim=1)
 
 
 def passed_along(value, axis, steps):
@@ -77,7 +108,7 @@
         combined = star_rows(upper_near, upper_far, full_now[0:2], rows_now[2:4])
         rows_now = jnp.where(group_index >= distance, combined, rows_now)
         if section_level + 1 < level_count:
-            full_now = lax.all_gather(rows_now, "blk", axis=1, tiled=True)
+            full_now = assign_files(rows_now)
     return rows_now[None]
 
 

time: 786 us -> 725 us (0.922); the launches traced: 784 us -> 714 us
  waiting for transfers between devices: 600 us -> 497 us
  starting transfers between devices: 35.1 us -> 61.9 us
  local copies, waits for them, and re-layouts: 13.7 us -> 29.9 us
    all_gather x6 -> x1, waiting for transfers between devices: 209 us -> 33.6 us  [on_device(): full_now = lax.all_gather(rows_now, 'blk', axis=1, tiled=True)]
    ppermute x0 -> x15, waiting for transfers between devices: none -> 99.5 us  [the longest x10 99.5 us: wrap_series_all(): f_next = jax.lax.ppermute(f_next, link_axis, so_far_all)]
    ppermute x6, waiting for transfers between devices: 347 us -> 320 us  [passed_along(): lax.ppermute(value, axis, [(source, source + steps) for source in range(f...]
    ppermute x0 -> x15, starting transfers between devices: none -> 16.4 us  [the longest x5 15.6 us: wrap_series_all(): frame_out = jax.lax.ppermute(frame_out, link_axis, pool)]
    dynamic_update_slice x0 -> x15, local copies, waits for them, and re-layouts: none -> 10.9 us  [the longest x10 7.29 us: wrap_series_all(): lax.dynamic_update_slice_in_dim(z1, f_next, (long_array - c) % d_next * n...]
    ppermute x6, starting transfers between devices: 22 us -> 32.6 us  [passed_along(): lax.ppermute(value, axis, [(source, source + steps) for source in range(f...]
  transfers between devices with their start and end apart: 16 -> 26, of which waited for: 15 -> 20; matrix products, arithmetic and copies ran while one was open for 0% -> 1% of each run, Pallas kernels for 0% -> 0%
where the time goes in v1:
time: 725 us; the launch traced here: 714 us
  waiting for transfers between devices  497 us (69%)
  matrix products  79.1 us (11%)
  starting transfers between devices  61.9 us (9%)
  local copies, waits for them, and re-layouts  29.9 us (4%)
  blocking collectives  23.6 us (3%)
  between operations  14.2 us (2%)
  other arithmetic  7.64 us (1%)
    ppermute x6, waiting for transfers between devices, passed_along(): lax.ppermute(value, axis, [(source, source + steps) for source in range(f...  320 us
    ppermute x10, waiting for transfers between devices, wrap_series_all(): f_next = jax.lax.ppermute(f_next, link_axis, so_far_all)  99.5 us
    dot_general x70, matrix products, times_f32(): return jnp.dot(left_op, right_op, preferred_element_type=jnp.float32)  75.4 us
    all_gather x1, waiting for transfers between devices, on_device(): full_now = lax.all_gather(rows_now, 'blk', axis=1, tiled=True)  33.6 us
    ppermute x6, starting transfers between devices, passed_along(): lax.ppermute(value, axis, [(source, source + steps) for source in range(f...  32.6 us
    all_gather x1, waiting for transfers between devices, on_device(): lax.all_gather(jnp.stack([refl_rows, tran_rows], axis=1), 'blk', axis=2,...  30.2 us
    all_to_all x1, blocking collectives, on_device(): lax.all_to_all(mode_matrix, 'layer', split_axis=0, concat_axis=1, tiled=T...  23.6 us
    ppermute x5, starting transfers between devices, wrap_series_all(): frame_out = jax.lax.ppermute(frame_out, link_axis, pool)  15.6 us
  transfers between devices with their start and end apart: 26, of which 20 were waited for; matrix products, arithmetic and copies ran while one was open for 1% of the time, Pallas kernels for 0%

profile of v1, /device:TPU:16, one launch (start us, length us, event | category | flops | bytes accessed | tf_op | source)
XLA Modules:
  0.0 713.5 jit_solution(448048660947568460)
XLA Ops:
  6.5 23.6 %all_to_all.44 = bf16[128,8,128]{2,1,0:T(8,128)(2,1)S(1)} all-to-all(bf16[128,8,128]{2,1,0:T(8,128)(2,1)} %param.3), channel_id=1, replica_groups=mesh['layer'=64,'blk'=4] {'layer'}, dimensions={0} | all-to-all | bytes 524288 | tf_op jit(solution)/shard_map/all_to_all | solution.py:71
  32.3 6.5 all-to-all-start.1
  46.5 6.4 all-to-all-start.2
  53.0 7.5 %all-to-all-done.2 = bf16[64,2,8]{2,1,0:T(2,128)(2,1)S(1)} async-done(((bf16[64,2,8]{2,1,0:T(2,128)(2,1)}), bf16[64,2,8]{2,1,0:T(2,128)(2,1)S(1)}, u32[]{:S(2)}, u32[]{:S(2)}) %all-to-all-start.2) | async-done | bytes 2080 | tf_op jit(solution)/shard_map/all_to_all | solution.py:72
  65.4 30.2 %all-gather.6.cloned.1.call-done = bf16[2,2,512,512]{3,2,0,1:T(8,128)(2,1)} async-done(((bf16[2,2,128,512]{3,2,0,1:T(8,128)(2,1)}), bf16[2,2,512,512]{3,2,0,1:T(8,128)(2,1)}) %all-gather.6.cloned.1.call-update) | async-done | bytes 2097168 | tf_op jit(solution)/shard_map/all_gather | solution.py:94
  101.8 33.6 %all-gather.8.cloned.1.call-done = bf16[4,512,512]{2,1,0:T(8,128)(2,1)} async-done(((bf16[4,128,512]{2,1,0:T(8,128)(2,1)}), bf16[4,512,512]{2,1,0:T(8,128)(2,1)}) %all-gather.8.cloned.1.call-update) | async-done | bytes 2097168 | tf_op jit(solution)/shard_map/all_gather | solution.py:100
  137.3 27.8 %collective-permute-done = bf16[4,512,512]{2,1,0:T(8,128)(2,1)} collective-permute-done((bf16[4,512,512]{2,1,0:T(8,128)(2,1)}, bf16[4,512,512]{2,1,0:T(8,128)(2,1)}, u32[]{:S(2)}, u32[]{:S(2)}) %collective-permute-start) | collective-permute-done | bytes 2097184 | tf_op jit(solution)/shard_map/ppermute | solution.py:44
  182.3 9.0 %collective-permute-done.1 = bf16[4,128,512]{2,1,0:T(8,128)(2,1)} collective-permute-done((bf16[4,128,512]{2,1,0:T(8,128)(2,1)S(1)}, bf16[4,128,512]{2,1,0:T(8,128)(2,1)}, u32[]{:S(2)}, u32[]{:S(2)}) %collective-permute-start.1) | collective-permute-done | bytes 524320 | tf_op jit(solution)/shard_map/ppermute | solution.py:26
  193.5 9.3 %collective-permute-done.3 = bf16[4,128,512]{2,1,0:T(8,128)(2,1)} collective-permute-done((bf16[4,128,512]{2,1,0:T(8,128)(2,1)}, bf16[4,128,512]{2,1,0:T(8,128)(2,1)}, u32[]{:S(2)}, u32[]{:S(2)}) %collective-permute-start.3) | collective-permute-done | bytes 524320 | tf_op jit(solution)/shard_map/ppermute | solution.py:26
  209.7 42.7 %collective-permute-done.4 = bf16[4,512,512]{2,1,0:T(8,128)(2,1)} collective-permute-done((bf16[4,512,512]{2,1,0:T(8,128)(2,1)S(1)}, bf16[4,512,512]{2,1,0:T(8,128)(2,1)}, u32[]{:S(2)}, u32[]{:S(2)}) %collective-permute-start.4) | collective-permute-done | bytes 2097184 | tf_op jit(solution)/shard_map/ppermute | solution.py:44
  270.4 8.9 %collective-permute-done.5 = bf16[4,128,512]{2,1,0:T(8,128)(2,1)S(1)} collective-permute-done((bf16[4,128,512]{2,1,0:T(8,128)(2,1)S(1)}, bf16[4,128,512]{2,1,0:T(8,128)(2,1)S(1)}, u32[]{:S(2)}, u32[]{:S(2)}) %collective-permute-start.5) | collective-permute-done | bytes 524320 | tf_op jit(solution)/shard_map/ppermute | solution.py:26
  280.9 8.7 %collective-permute-done.7 = bf16[4,128,512]{2,1,0:T(8,128)(2,1)S(1)} collective-permute-done((bf16[4,128,512]{2,1,0:T(8,128)(2,1)S(1)}, bf16[4,128,512]{2,1,0:T(8,128)(2,1)S(1)}, u32[]{:S(2)}, u32[]{:S(2)}) %collective-permute-start.7) | collective-permute-done | bytes 524320 | tf_op jit(solution)/shard_map/ppermute | solution.py:26
  290.4 10.3 %collective-permute-start.8 = (bf16[4,512,512]{2,1,0:T(8,128)(2,1)}, bf16[4,512,512]{2,1,0:T(8,128)(2,1)}, u32[]{:S(2)}, u32[]{:S(2)}) collective-permute-start(bf16[4,512,512]{2,1,0:T(8,128)(2,1)} %constant_dynamic-update-slice_fusion.12), channel_id=1, source_target_pairs={{0,16},{4,20},{8,24},{12,28},{16,32},{20,36},{24,40},{28,44},{32,4... | collective-permute-start | bytes 6291464 | tf_op jit(solution)/shard_map/ppermute | solution.py:44
  300.7 80.3 %collective-permute-done.8 = bf16[4,512,512]{2,1,0:T(8,128)(2,1)} collective-permute-done((bf16[4,512,512]{2,1,0:T(8,128)(2,1)}, bf16[4,512,512]{2,1,0:T(8,128)(2,1)}, u32[]{:S(2)}, u32[]{:S(2)}) %collective-permute-start.8) | collective-permute-done | bytes 2097184 | tf_op jit(solution)/shard_map/ppermute | solution.py:44
  398.9 11.8 %collective-permute-done.9 = bf16[4,128,512]{2,1,0:T(8,128)(2,1)S(1)} collective-permute-done((bf16[4,128,512]{2,1,0:T(8,128)(2,1)S(1)}, bf16[4,128,512]{2,1,0:T(8,128)(2,1)S(1)}, u32[]{:S(2)}, u32[]{:S(2)}) %collective-permute-start.9) | collective-permute-done | bytes 524320 | tf_op jit(solution)/shard_map/ppermute | solution.py:26
  412.4 12.5 %collective-permute-done.11 = bf16[4,128,512]{2,1,0:T(8,128)(2,1)S(1)} collective-permute-done((bf16[4,128,512]{2,1,0:T(8,128)(2,1)S(1)}, bf16[4,128,512]{2,1,0:T(8,128)(2,1)S(1)}, u32[]{:S(2)}, u32[]{:S(2)}) %collective-permute-start.11) | collective-permute-done | bytes 524320 | tf_op jit(solution)/shard_map/ppermute | solution.py:26
  425.7 11.4 %collective-permute-start.12 = (bf16[4,512,512]{2,1,0:T(8,128)(2,1)}, bf16[4,512,512]{2,1,0:T(8,128)(2,1)}, u32[]{:S(2)}, u32[]{:S(2)}) collective-permute-start(bf16[4,512,512]{2,1,0:T(8,128)(2,1)} %constant_dynamic-update-slice_fusion.8), channel_id=1, source_target_pairs={{0,32},{4,36},{8,40},{12,44},{16,48},{20,52},{24,56},{28,60},{32,6... | collective-permute-start | bytes 6291464 | tf_op jit(solution)/shard_map/ppermute | solution.py:44
  437.1 87.1 %collective-permute-done.12 = bf16[4,512,512]{2,1,0:T(8,128)(2,1)} collective-permute-done((bf16[4,512,512]{2,1,0:T(8,128)(2,1)}, bf16[4,512,512]{2,1,0:T(8,128)(2,1)}, u32[]{:S(2)}, u32[]{:S(2)}) %collective-permute-start.12) | collective-permute-done | bytes 2097184 | tf_op jit(solution)/shard_map/ppermute | solution.py:44
  542.2 8.9 %collective-permute-done.13 = bf16[4,128,512]{2,1,0:T(8,128)(2,1)S(1)} collective-permute-done((bf16[4,128,512]{2,1,0:T(8,128)(2,1)S(1)}, bf16[4,128,512]{2,1,0:T(8,128)(2,1)S(1)}, u32[]{:S(2)}, u32[]{:S(2)}) %collective-permute-start.13) | collective-permute-done | bytes 524320 | tf_op jit(solution)/shard_map/ppermute | solution.py:26
  552.7 8.7 %collective-permute-done.15 = bf16[4,128,512]{2,1,0:T(8,128)(2,1)S(1)} collective-permute-done((bf16[4,128,512]{2,1,0:T(8,128)(2,1)S(1)}, bf16[4,128,512]{2,1,0:T(8,128)(2,1)S(1)}, u32[]{:S(2)}, u32[]{:S(2)}) %collective-permute-start.15) | collective-permute-done | bytes 524320 | tf_op jit(solution)/shard_map/ppermute | solution.py:26
  564.2 41.6 %collective-permute-done.16 = bf16[4,512,512]{2,1,0:T(8,128)(2,1)} collective-permute-done((bf16[4,512,512]{2,1,0:T(8,128)(2,1)}, bf16[4,512,512]{2,1,0:T(8,128)(2,1)}, u32[]{:S(2)}, u32[]{:S(2)}) %collective-permute-start.16) | collective-permute-done | bytes 2097184 | tf_op jit(solution)/shard_map/ppermute | solution.py:44
  623.1 11.5 %collective-permute-done.17 = bf16[4,128,512]{2,1,0:T(8,128)(2,1)S(1)} collective-permute-done((bf16[4,128,512]{2,1,0:T(8,128)(2,1)S(1)}, bf16[4,128,512]{2,1,0:T(8,128)(2,1)S(1)}, u32[]{:S(2)}, u32[]{:S(2)}) %collective-permute-start.17) | collective-permute-done | bytes 524320 | tf_op jit(solution)/shard_map/ppermute | solution.py:26
  634.7 10.3 %collective-permute-done.19 = bf16[4,128,512]{2,1,0:T(8,128)(2,1)S(1)} collective-permute-done((bf16[4,128,512]{2,1,0:T(8,128)(2,1)S(1)}, bf16[4,128,512]{2,1,0:T(8,128)(2,1)S(1)}, u32[]{:S(2)}, u32[]{:S(2)}) %collective-permute-start.19) | collective-permute-done | bytes 524320 | tf_op jit(solution)/shard_map/ppermute | solution.py:26
  646.4 40.4 %collective-permute-done.20 = bf16[4,512,512]{2,1,0:T(8,128)(2,1)} collective-permute-done((bf16[4,512,512]{2,1,0:T(8,128)(2,1)S(1)}, bf16[4,512,512]{2,1,0:T(8,128)(2,1)}, u32[]{:S(2)}, u32[]{:S(2)}) %collective-permute-start.20) | collective-permute-done | bytes 2097184 | tf_op jit(solution)/shard_map/ppermute | solution.py:44
  (203 shorter events, 150.4 us)
Async XLA Ops:
  6.5 54.4 %all-gather.4.cloned.1.call-start = ((), (), s32[]{:S(2)}) async-start(), calls=%async_computation.3 | async-start | bytes 1310720 | tf_op jit(solution)/shard_map/all_gather | solution.py:80
  32.3 14.2 %all-to-all-start.1 = ((bf16[64,2,8]{2,1,0:T(2,128)(2,1)}), bf16[64,2,8]{2,1,0:T(2,128)(2,1)S(1)}, u32[]{:S(2)}, u32[]{:S(2)}) async-start(bf16[64,2,8]{2,1,0:T(2,128)(2,1)} %bitcast.3), calls=%async_computation.1 | async-start | bytes 65536 | tf_op jit(solution)/shard_map/all_to_all | solution.py:73
  46.5 14.1 %all-to-all-start.2 = ((bf16[64,2,8]{2,1,0:T(2,128)(2,1)}), bf16[64,2,8]{2,1,0:T(2,128)(2,1)S(1)}, u32[]{:S(2)}, u32[]{:S(2)}) async-start(bf16[64,2,8]{2,1,0:T(2,128)(2,1)} %bitcast.6), calls=%async_computation.2 | async-start | bytes 65536 | tf_op jit(solution)/shard_map/all_to_all | solution.py:72
  52.8 42.8 %all-gather.6.cloned.1.call-start = ((), (), s32[]{:S(2)}) async-start(), calls=%async_computation.4 | async-start | bytes 2621440 | tf_op jit(solution)/shard_map/all_gather | solution.py:94
  65.4 70.0 %all-gather.8.cloned.1.call-start = ((), (), s32[]{:S(2)}) async-start(), calls=%async_computation.5 | async-start | bytes 2621440 | tf_op jit(solution)/shard_map/all_gather | solution.py:100
  135.3 29.8 %collective-permute-start = (bf16[4,512,512]{2,1,0:T(8,128)(2,1)}, bf16[4,512,512]{2,1,0:T(8,128)(2,1)}, u32[]{:S(2)}, u32[]{:S(2)}) collective-permute-start(bf16[4,512,512]{2,1,0:T(8,128)(2,1)} %all-gather.8.cloned.1.call-done), channel_id=1, source_target_pairs={{0,4},{4,8},{8,12},{12,16},{16,20},{20,24},{24,28},{28,32},{32,36}... | collective-permute-start | bytes 6291464 | tf_op jit(solution)/shard_map/ppermute | solution.py:44
  179.0 12.3 %collective-permute-start.1 = (bf16[4,128,512]{2,1,0:T(8,128)(2,1)S(1)}, bf16[4,128,512]{2,1,0:T(8,128)(2,1)}, u32[]{:S(2)}, u32[]{:S(2)}) collective-permute-start(bf16[4,128,512]{2,1,0:T(8,128)(2,1)S(1)} %get-tuple-element.14), channel_id=1, source_target_pairs={{0,1},{1,2},{2,3},{3,0},{4,5},{5,6},{6,7},{7,4},{8,9},{9,10},{10,1... | collective-permute-start | bytes 1572872 | tf_op jit(solution)/shard_map/ppermute | solution.py:26
  179.6 12.8 %collective-permute-start.2 = (bf16[4,128,512]{2,1,0:T(8,128)(2,1)S(1)}, bf16[4,128,512]{2,1,0:T(8,128)(2,1)}, u32[]{:S(2)}, u32[]{:S(2)}) collective-permute-start(bf16[4,128,512]{2,1,0:T(8,128)(2,1)S(1)} %get-tuple-element.14), channel_id=1, source_target_pairs={{0,3},{1,0},{2,1},{3,2},{4,7},{5,4},{6,5},{7,6},{8,11},{9,8},{10,9... | collective-permute-start | bytes 1572872 | tf_op jit(solution)/shard_map/ppermute | solution.py:31
  191.3 11.5 %collective-permute-start.3 = (bf16[4,128,512]{2,1,0:T(8,128)(2,1)}, bf16[4,128,512]{2,1,0:T(8,128)(2,1)}, u32[]{:S(2)}, u32[]{:S(2)}) collective-permute-start(bf16[4,128,512]{2,1,0:T(8,128)(2,1)} %collective-permute-done.1), channel_id=1, source_target_pairs={{0,1},{1,2},{2,3},{3,0},{4,5},{5,6},{6,7},{7,4},{8,9},{9,10},{10,1... | collective-permute-start | bytes 1572872 | tf_op jit(solution)/shard_map/ppermute | solution.py:26
  203.9 48.4 %collective-permute-start.4 = (bf16[4,512,512]{2,1,0:T(8,128)(2,1)S(1)}, bf16[4,512,512]{2,1,0:T(8,128)(2,1)}, u32[]{:S(2)}, u32[]{:S(2)}) collective-permute-start(bf16[4,512,512]{2,1,0:T(8,128)(2,1)S(1)} %constant_dynamic-update-slice_fusion.16), channel_id=1, source_target_pairs={{0,8},{4,12},{8,16},{12,20},{16,24},{20,28},{24,32},{28,36},{32,40... | collective-permute-start | bytes 6291464 | tf_op jit(solution)/shard_map/ppermute | solution.py:44
  267.1 12.2 %collective-permute-start.5 = (bf16[4,128,512]{2,1,0:T(8,128)(2,1)S(1)}, bf16[4,128,512]{2,1,0:T(8,128)(2,1)S(1)}, u32[]{:S(2)}, u32[]{:S(2)}) collective-permute-start(bf16[4,128,512]{2,1,0:T(8,128)(2,1)S(1)} %get-tuple-element.12), channel_id=1, source_target_pairs={{0,1},{1,2},{2,3},{3,0},{4,5},{5,6},{6,7},{7,4},{8,9},{9,10},{10,1... | collective-permute-start | bytes 1572872 | tf_op jit(solution)/shard_map/ppermute | solution.py:26
  267.1 12.9 %collective-permute-start.6 = (bf16[4,128,512]{2,1,0:T(8,128)(2,1)S(1)}, bf16[4,128,512]{2,1,0:T(8,128)(2,1)S(1)}, u32[]{:S(2)}, u32[]{:S(2)}) collective-permute-start(bf16[4,128,512]{2,1,0:T(8,128)(2,1)S(1)} %get-tuple-element.12), channel_id=1, source_target_pairs={{0,3},{1,0},{2,1},{3,2},{4,7},{5,4},{6,5},{7,6},{8,11},{9,8},{10,9... | collective-permute-start | bytes 1572872 | tf_op jit(solution)/shard_map/ppermute | solution.py:31
  279.2 10.4 %collective-permute-start.7 = (bf16[4,128,512]{2,1,0:T(8,128)(2,1)S(1)}, bf16[4,128,512]{2,1,0:T(8,128)(2,1)S(1)}, u32[]{:S(2)}, u32[]{:S(2)}) collective-permute-start(bf16[4,128,512]{2,1,0:T(8,128)(2,1)S(1)} %collective-permute-done.5), channel_id=1, source_target_pairs={{0,1},{1,2},{2,3},{3,0},{4,5},{5,6},{6,7},{7,4},{8,9},{9,10},{10,1... | collective-permute-start | bytes 1572872 | tf_op jit(solution)/shard_map/ppermute | solution.py:26
  290.4 90.6 %collective-permute-start.8 = (bf16[4,512,512]{2,1,0:T(8,128)(2,1)}, bf16[4,512,512]{2,1,0:T(8,128)(2,1)}, u32[]{:S(2)}, u32[]{:S(2)}) collective-permute-start(bf16[4,512,512]{2,1,0:T(8,128)(2,1)} %constant_dynamic-update-slice_fusion.12), channel_id=1, source_target_pairs={{0,16},{4,20},{8,24},{12,28},{16,32},{20,36},{24,40},{28,44},{32,4... | collective-permute-start | bytes 6291464 | tf_op jit(solution)/shard_map/ppermute | solution.py:44
  395.7 15.0 %collective-permute-start.9 = (bf16[4,128,512]{2,1,0:T(8,128)(2,1)S(1)}, bf16[4,128,512]{2,1,0:T(8,128)(2,1)S(1)}, u32[]{:S(2)}, u32[]{:S(2)}) collective-permute-start(bf16[4,128,512]{2,1,0:T(8,128)(2,1)S(1)} %get-tuple-element.10), channel_id=1, source_target_pairs={{0,1},{1,2},{2,3},{3,0},{4,5},{5,6},{6,7},{7,4},{8,9},{9,10},{10,1... | collective-permute-start | bytes 1572872 | tf_op jit(solution)/shard_map/ppermute | solution.py:26
  395.7 15.8 %collective-permute-start.10 = (bf16[4,128,512]{2,1,0:T(8,128)(2,1)S(1)}, bf16[4,128,512]{2,1,0:T(8,128)(2,1)S(1)}, u32[]{:S(2)}, u32[]{:S(2)}) collective-permute-start(bf16[4,128,512]{2,1,0:T(8,128)(2,1)S(1)} %get-tuple-element.10), channel_id=1, source_target_pairs={{0,3},{1,0},{2,1},{3,2},{4,7},{5,4},{6,5},{7,6},{8,11},{9,8},{10,9... | collective-permute-start | bytes 1572872 | tf_op jit(solution)/shard_map/ppermute | solution.py:31
  410.7 14.1 %collective-permute-start.11 = (bf16[4,128,512]{2,1,0:T(8,128)(2,1)S(1)}, bf16[4,128,512]{2,1,0:T(8,128)(2,1)S(1)}, u32[]{:S(2)}, u32[]{:S(2)}) collective-permute-start(bf16[4,128,512]{2,1,0:T(8,128)(2,1)S(1)} %collective-permute-done.9), channel_id=1, source_target_pairs={{0,1},{1,2},{2,3},{3,0},{4,5},{5,6},{6,7},{7,4},{8,9},{9,10},{10,1... | collective-permute-start | bytes 1572872 | tf_op jit(solution)/shard_map/ppermute | solution.py:26
  425.7 98.6 %collective-permute-start.12 = (bf16[4,512,512]{2,1,0:T(8,128)(2,1)}, bf16[4,512,512]{2,1,0:T(8,128)(2,1)}, u32[]{:S(2)}, u32[]{:S(2)}) collective-permute-start(bf16[4,512,512]{2,1,0:T(8,128)(2,1)} %constant_dynamic-update-slice_fusion.8), channel_id=1, source_target_pairs={{0,32},{4,36},{8,40},{12,44},{16,48},{20,52},{24,56},{28,60},{32,6... | collective-permute-start | bytes 6291464 | tf_op jit(solution)/shard_map/ppermute | solution.py:44
  538.9 12.1 %collective-permute-start.13 = (bf16[4,128,512]{2,1,0:T(8,128)(2,1)S(1)}, bf16[4,128,512]{2,1,0:T(8,128)(2,1)S(1)}, u32[]{:S(2)}, u32[]{:S(2)}) collective-permute-start(bf16[4,128,512]{2,1,0:T(8,128)(2,1)S(1)} %get-tuple-element.8), channel_id=1, source_target_pairs={{0,1},{1,2},{2,3},{3,0},{4,5},{5,6},{6,7},{7,4},{8,9},{9,10},{10,1... | collective-permute-start | bytes 1572872 | tf_op jit(solution)/shard_map/ppermute | solution.py:26
  538.9 12.9 %collective-permute-start.14 = (bf16[4,128,512]{2,1,0:T(8,128)(2,1)S(1)}, bf16[4,128,512]{2,1,0:T(8,128)(2,1)S(1)}, u32[]{:S(2)}, u32[]{:S(2)}) collective-permute-start(bf16[4,128,512]{2,1,0:T(8,128)(2,1)S(1)} %get-tuple-element.8), channel_id=1, source_target_pairs={{0,3},{1,0},{2,1},{3,2},{4,7},{5,4},{6,5},{7,6},{8,11},{9,8},{10,9... | collective-permute-start | bytes 1572872 | tf_op jit(solution)/shard_map/ppermute | solution.py:31
  562.3 43.6 %collective-permute-start.16 = (bf16[4,512,512]{2,1,0:T(8,128)(2,1)}, bf16[4,512,512]{2,1,0:T(8,128)(2,1)}, u32[]{:S(2)}, u32[]{:S(2)}) collective-permute-start(bf16[4,512,512]{2,1,0:T(8,128)(2,1)} %constant_dynamic-update-slice_fusion.4), channel_id=1, source_target_pairs={{0,64},{4,68},{8,72},{12,76},{16,80},{20,84},{24,88},{28,92},{32,9... | collective-permute-start | bytes 6291464 | tf_op jit(solution)/shard_map/ppermute | solution.py:44
  619.8 14.8 %collective-permute-start.17 = (bf16[4,128,512]{2,1,0:T(8,128)(2,1)S(1)}, bf16[4,128,512]{2,1,0:T(8,128)(2,1)S(1)}, u32[]{:S(2)}, u32[]{:S(2)}) collective-permute-start(bf16[4,128,512]{2,1,0:T(8,128)(2,1)S(1)} %get-tuple-element.6), channel_id=1, source_target_pairs={{0,1},{1,2},{2,3},{3,0},{4,5},{5,6},{6,7},{7,4},{8,9},{9,10},{10,1... | collective-permute-start | bytes 1572872 | tf_op jit(solution)/shard_map/ppermute | solution.py:26
  619.9 14.8 %collective-permute-start.18 = (bf16[4,128,512]{2,1,0:T(8,128)(2,1)S(1)}, bf16[4,128,512]{2,1,0:T(8,128)(2,1)S(1)}, u32[]{:S(2)}, u32[]{:S(2)}) collective-permute-start(bf16[4,128,512]{2,1,0:T(8,128)(2,1)S(1)} %get-tuple-element.6), channel_id=1, source_target_pairs={{0,3},{1,0},{2,1},{3,2},{4,7},{5,4},{6,5},{7,6},{8,11},{9,8},{10,9... | collective-permute-start | bytes 1572872 | tf_op jit(solution)/shard_map/ppermute | solution.py:31
  645.1 41.7 %collective-permute-start.20 = (bf16[4,512,512]{2,1,0:T(8,128)(2,1)S(1)}, bf16[4,512,512]{2,1,0:T(8,128)(2,1)}, u32[]{:S(2)}, u32[]{:S(2)}) collective-permute-start(bf16[4,512,512]{2,1,0:T(8,128)(2,1)S(1)} %constant_dynamic-update-slice_fusion), channel_id=1, source_target_pairs={{0,128},{4,132},{8,136},{12,140},{16,144},{20,148},{24,152},{28,15... | collective-permute-start | bytes 6291464 | tf_op jit(solution)/shard_map/ppermute | solution.py:44
  (29 other events, 164.8 us)
Sparse Core Ops, SparseCore 0:
  31.0 25.5 all-gather.3
  65.5 30.1 all-gather.5
  101.9 33.4 all-gather.7
